TPU v7x, 128 devices: a whole 4x4x4 slice. The times are simulated.
128 devices in a mesh: frame: 32 (over z, x_hi, y), head: 4 (over x_lo, core).
Axes of the slice: x: 4 (x_hi: 2, x_lo: 2; x = x_hi * 2 + x_lo), y: 4, z: 4, core: 2. Of those that a mesh axis runs over, the one named last changes fastest.
Arguments:
- queries: bfloat16 [24576, 5120], P('frame', 'head'), may hold values from -6.4 to 6.4
- keys: bfloat16 [24576, 5120], P('frame', 'head'), may hold values from -6.4 to 6.4
- values: bfloat16 [24576, 5120], P('frame', 'head'), may hold values from -6 to 6
- out_weight: bfloat16 [5120, 5120], P('head'), may hold values from -0.078125 to 0.078125
- sink_owner: int32 [32], replicated, may hold values from 0 to 31, each once
- frame_pos: int32 [32], P('frame'), may hold values from 0 to 93, as said below
Outputs:
- mixed: bfloat16 [24576, 5120], P('frame', 'head')
Inputs may be any that keep to these rules, and one draw needn't show every extreme that they name: `frame_pos`: strictly increasing, first entry 0, steps of 2 to 4. `sink_owner`: each number once.
All inputs are finite; a program needn't handle non-finite values.
Results may differ from a plain program's by a relative error of at most 0.01.
Values may be sent and summed in bfloat16 or wider, within the bound.
No kernel may reach another device: no remote copies, remote signals or barrier semaphores. Data moves between devices by JAX's collectives and lax.ppermute only.
A program may use at most 192 MiB of HBM per device.

v0:
```python
import jax
import jax.numpy as jnp
from jax import lax
from jax.sharding import PartitionSpec as P

HDIM = 128
GRID_W = 32


def shifted(array, axis, by):
    length = lax.axis_size(axis)
    pairs = [(i, i + by) for i in range(length) if 0 <= i + by < length]
    return lax.ppermute(array, axis, pairs)


def broadcast(value, axis, source):
    kept = jnp.where(lax.axis_index(axis) == source, value, 0).astype(value.dtype)
    return lax.psum(kept, axis)


def pair_angles(frame_value, count):
    half = HDIM // 2
    tdim = HDIM - 4 * (HDIM // 6)
    sdim = 2 * (HDIM // 6)
    tcount = tdim // 2
    scount = sdim // 2
    index = jnp.arange(half)
    findex = index.astype(jnp.float32)
    freq = jnp.where(
        index < tcount,
        jnp.power(10000.0, -2.0 * findex / tdim),
        jnp.where(
            index < tcount + scount,
            jnp.power(10000.0, -2.0 * (findex - tcount) / sdim),
            jnp.power(10000.0, -2.0 * (findex - tcount - scount) / sdim),
        ),
    )
    token = jnp.arange(count)
    row_pos = (token // GRID_W).astype(jnp.float32)[:, None]
    col_pos = (token % GRID_W).astype(jnp.float32)[:, None]
    frame_f = jnp.zeros((count, 1), jnp.float32) + frame_value.astype(jnp.float32)
    pos = jnp.where(
        index[None, :] < tcount,
        frame_f,
        jnp.where(index[None, :] < tcount + scount, row_pos, col_pos),
    )
    return pos * freq[None, :]


def rotate(block, angle):
    count = block.shape[0]
    heads_here = block.shape[1] // HDIM
    parts = block.astype(jnp.float32).reshape(count, heads_here, HDIM // 2, 2)
    cosine = jnp.cos(angle)[:, None, :]
    sine = jnp.sin(angle)[:, None, :]
    first = parts[..., 0] * cosine - parts[..., 1] * sine
    second = parts[..., 0] * sine + parts[..., 1] * cosine
    return (
        jnp.stack([first, second], axis=-1).reshape(count, heads_here * HDIM).astype(jnp.bfloat16)
    )


def attend_block(query, key_block, value_block):
    count = query.shape[0]
    heads_here = query.shape[1] // HDIM
    qh = query.reshape(count, heads_here, HDIM)
    kh = key_block.reshape(-1, heads_here, HDIM)
    vh = value_block.reshape(-1, heads_here, HDIM)
    scores = jnp.einsum("qhd,khd->hqk", qh, kh, preferred_element_type=jnp.float32) / jnp.sqrt(
        jnp.float32(HDIM)
    )
    peak = jnp.max(scores, axis=-1)
    weights = jnp.exp(scores - peak[..., None]).astype(jnp.bfloat16)
    total = jnp.sum(weights.astype(jnp.float32), axis=-1)
    partial_value = jnp.einsum("hqk,khd->hqd", weights, vh, preferred_element_type=jnp.float32)
    return (peak, total, partial_value)


def shards(queries, keys, values, out_weight, sink_owner, frame_pos):
    count = queries.shape[0]
    angle = pair_angles(frame_pos[0], count)
    rot_q = rotate(queries, angle)
    rot_k = rotate(keys, angle)
    place = lax.axis_index("frame")
    sink = sink_owner[0] % (lax.axis_size("frame") // 2)
    prev_k, prev_v = shifted((rot_k, values), "frame", 1)
    sink_k, sink_v = (broadcast(rot_k, "frame", sink), broadcast(values, "frame", sink))
    prev_used = (place >= 1) & (place - 1 != sink)
    sink_used = sink < place
    m_self, l_self, o_self = attend_block(rot_q, rot_k, values)
    m_prev, l_prev, o_prev = attend_block(rot_q, prev_k, prev_v)
    m_sink, l_sink, o_sink = attend_block(rot_q, sink_k, sink_v)
    top = jnp.maximum(m_self, jnp.where(prev_used, m_prev, m_self))
    top = jnp.maximum(top, jnp.where(sink_used, m_sink, m_self))
    c_self = jnp.exp(m_self - top)
    c_prev = jnp.where(prev_used, jnp.exp(m_prev - top), 0.0)
    c_sink = jnp.where(sink_used, jnp.exp(m_sink - top), 0.0)
    numer = o_self * c_self[..., None] + o_prev * c_prev[..., None] + o_sink * c_sink[..., None]
    denom = l_self * c_self + l_prev * c_prev + l_sink * c_sink
    attended = (
        jnp.transpose(numer / denom[..., None], (1, 0, 2)).reshape(count, -1).astype(jnp.bfloat16)
    )
    terms = jnp.dot(attended, out_weight, preferred_element_type=jnp.float32)
    mixed = lax.psum_scatter(terms.astype(jnp.bfloat16), "head", scatter_dimension=1, tiled=True)
    return mixed


def solution(mesh):
    in_specs = (
        P("frame", "head"),
        P("frame", "head"),
        P("frame", "head"),
        P("head", None),
        P(),
        P("frame"),
    )
    out_specs = P("frame", "head")
    return jax.shard_map(shards, mesh=mesh, in_specs=in_specs, out_specs=out_specs, check_vma=False)
```

profile of v0, /device:TPU:1, one launch (start us, length us, event | category | flops | bytes accessed | tf_op | source)
XLA Modules:
  0.0 553.0 jit_solution(17871531195031379992)
XLA Ops:
  6.5 5.4 collective-permute-start.1
  12.6 4.3 copy.19
  16.9 5.6 %reshape.273 = f32[768,10,64,2]{0,3,2,1:T(2,128)} reshape(f32[768,1280]{0,1:T(8,128)} %copy.19) | data formatting | bytes 7864320 | tf_op jit(solution)/shard_map/reshape | solution.py:53
  22.4 0.8 fusion.7
  23.2 7.0 %multiply_subtract_fusion = (bf16[768,10,64,1]{0,3,2,1:T(2,128)(2,1)S(1)}, bf16[768,10,64,1]{0,3,2,1:T(2,128)(2,1)S(1)}) fusion(f32[768,10,64,2]{0,3,2,1:T(2,128)} %reshape.273, f32[768,64]{0,1:T(8,128)S(1)} %get-tuple-element.16, f32[768,64]{0,1:T(8,128)S(1)} %get-tuple-element.15), kind=kLoop, calls=%fused_computation.20 | loop fusion | flops 3932160 | bytes 6291456 | tf_op jit(solution)/shard_map/sub | solution.py:56
  30.3 4.5 maximum_convert_fusion
  34.7 1.9 convert_element_type.83
  36.7 3.1 collective-permute-start
  39.9 2.7 copy.22
  42.6 1.6 broadcast_select_fusion.1
  44.2 1.4 broadcast_select_fusion
  45.6 4.0 copy.26
  50.3 5.2 convert_element_type.81
  55.5 4.3 copy.18
  59.8 5.6 %reshape.271 = f32[768,10,64,2]{0,3,2,1:T(2,128)} reshape(f32[768,1280]{0,1:T(8,128)} %copy.18) | data formatting | bytes 7864320 | tf_op jit(solution)/shard_map/reshape | solution.py:53
  65.4 7.0 %subtract_convert_fusion = (bf16[768,10,64,1]{0,3,2,1:T(2,128)(2,1)S(1)}, bf16[768,10,64,1]{0,3,2,1:T(2,128)(2,1)S(1)}) fusion(f32[768,10,64,2]{0,3,2,1:T(2,128)} %reshape.271, f32[768,64]{0,1:T(8,128)S(1)} %get-tuple-element.16, f32[768,64]{0,1:T(8,128)S(1)} %get-tuple-element.15), kind=kLoop, calls=%fused_computation.22 | loop fusion | flops 3932160 | bytes 6291456 | tf_op jit(solution)/shard_map/convert.2
  72.4 5.7 %pad_maximum_fusion = bf16[768,10,64,2]{0,3,2,1:T(2,128)(2,1)} fusion(bf16[768,10,64,1]{0,3,2,1:T(2,128)(2,1)S(1)} %get-tuple-element.12, bf16[768,10,64,1]{0,3,2,1:T(2,128)(2,1)S(1)} %get-tuple-element.11), kind=kLoop, calls=%fused_computation.18 | loop fusion | flops 3932160 | bytes 3932160 | tf_op jit(solution)/shard_map/stack | solution.py:59
  78.1 4.5 convert_element_type.79
  82.6 12.7 %multiply_reduce_fusion.2 = (f32[10,768]{1,0:T(8,128)S(1)}, f32[10,768,768]{1,2,0:T(8,128)}) fusion(bf16[768,10,128]{0,2,1:T(8,128)(2,1)S(1)} %convert_element_type.79, bf16[768,10,128]{0,2,1:T(8,128)(2,1)} %convert_element_type.81), kind=kOutput, calls=%fused_computation.8 | convolution fusion | flops 1521738240 | bytes 27555840 | tf_op jit(solution)/shard_map/qhd,khd->hqk/dot_general | solution.py:69
  95.3 10.6 %convert_reduce_fusion.2 = f32[10,768]{1,0:T(8,128)} fusion(f32[10,768]{1,0:T(8,128)S(1)} %get-tuple-element.19, f32[10,768,768]{1,2,0:T(8,128)} %get-tuple-element.20), kind=kLoop, calls=%fused_computation.2 | loop fusion | flops 29483520 | bytes 23654400 | tf_op jit(solution)/shard_map/reduce_sum | solution.py:74
  105.9 14.8 %fusion.4 = f32[10,768,128]{1,2,0:T(8,128)} fusion(bf16[768,10,128]{0,2,1:T(8,128)(2,1)} %bitcast.105, f32[10,768,768]{1,2,0:T(8,128)} %get-tuple-element.20, f32[10,768]{1,0:T(8,128)S(1)} %get-tuple-element.19), kind=kOutput, calls=%fused_computation.25 | convolution fusion | flops 1527644160 | bytes 29521920 | tf_op jit(solution)/shard_map/hqk,khd->hqd/dot_general | solution.py:75
  120.7 4.0 copy.28
  124.7 12.7 %multiply_reduce_fusion.1 = (f32[10,768]{1,0:T(8,128)S(1)}, f32[10,768,768]{1,2,0:T(8,128)}) fusion(bf16[768,10,128]{0,2,1:T(8,128)(2,1)S(1)} %convert_element_type.79, bf16[768,10,128]{0,2,1:T(8,128)(2,1)} %bitcast.5), kind=kOutput, calls=%fused_computation.7 | convolution fusion | flops 1521738240 | bytes 27555840 | tf_op jit(solution)/shard_map/qhd,khd->hqk/dot_general | solution.py:69
  137.4 10.9 %convert_reduce_fusion.1 = f32[10,768]{1,0:T(8,128)} fusion(f32[10,768]{1,0:T(8,128)S(1)} %get-tuple-element.21, f32[10,768,768]{1,2,0:T(8,128)} %get-tuple-element.22), kind=kLoop, calls=%fused_computation.1 | loop fusion | flops 29483520 | bytes 23654400 | tf_op jit(solution)/shard_map/reduce_sum | solution.py:74
  148.3 246.6 %all-reduce.3.cloned.1.call-done = (bf16[768,10,128]{0,2,1:T(8,128)(2,1)}, bf16[768,10,128]{2,0,1:T(8,128)(2,1)}) async-done(((bf16[768,10,128]{0,2,1:T(8,128)(2,1)}, bf16[768,10,128]{2,0,1:T(8,128)(2,1)}), (bf16[768,10,128]{0,2,1:T(8,128)(2,1)}, bf16[768,10,128]{2,0,1:T(8,128)(2,1)})) %all-reduce.3.cloned.1.call-update) | async-done | bytes 3932176 | tf_op jit(solution)/shard_map/psum | solution.py:18
  394.9 5.4 multiply_reduce_fusion
  400.3 7.2 %convert_reduce_fusion = f32[10,768]{1,0:T(8,128)} fusion(f32[10,768]{1,0:T(8,128)} %get-tuple-element.17, f32[10,768,768]{1,2,0:T(8,128)S(1)} %get-tuple-element.18), kind=kLoop, calls=%fused_computation | loop fusion | flops 29483520 | bytes 23654400 | tf_op jit(solution)/shard_map/reduce_sum | solution.py:74
  407.5 1.4 copy-done
  408.9 10.0 %fusion.5 = f32[10,768,128]{1,2,0:T(8,128)S(1)} fusion(bf16[768,10,128]{0,2,1:T(8,128)(2,1)S(1)} %copy-done.4, f32[10,768,768]{1,2,0:T(8,128)} %copy-done, f32[10,768]{1,0:T(8,128)} %get-tuple-element.17), kind=kOutput, calls=%fused_computation.26 | convolution fusion | flops 1527644160 | bytes 29521920 | tf_op jit(solution)/shard_map/hqk,khd->hqd/dot_general | solution.py:75
  419.0 11.8 %fusion.2 = bf16[768,10,128]{0,2,1:T(8,128)(2,1)} fusion(f32[10,768,128]{1,2,0:T(8,128)S(1)} %fusion.5, f32[10,768,128]{1,2,0:T(8,128)S(1)} %copy-done.3, bf16[768,10,128]{0,2,1:T(8,128)(2,1)} %bitcast.108, f32[768,10]{0,1:T(8,128)S(1)} %get-tuple-element.7, f32[768,10]{0,1:T(8,128)S(1)} %get-tuple-element.10, f32[768,10]{0,1:T(8,128)S(1)} %get-tuple-element.9, ...), kind=kOutput, calls=%fused_computation.14 | convolution fusion | flops 1534525440 | bytes 35543040 | tf_op jit(solution)/shard_map/hqk,khd->hqd/dot_general | solution.py:75
  430.8 17.9 %convolution_convert_fusion = bf16[768,5120]{1,0:T(8,128)(2,1)} fusion(bf16[768,1280]{0,1:T(8,128)(2,1)} %bitcast.112, bf16[1280,5120]{1,0:T(8,128)(2,1)} %param.9), kind=kOutput, calls=%fused_computation.9 | convolution fusion | flops 10070261760 | bytes 22937600 | tf_op jit(solution)/shard_map/dot_general | solution.py:103
  448.7 97.0 %reduce-scatter.2.cloned.1.call-done = bf16[768,1280]{1,0:T(8,128)(2,1)} async-done(((bf16[768,5120]{1,0:T(8,128)(2,1)}), bf16[768,1280]{1,0:T(8,128)(2,1)}) %reduce-scatter.2.cloned.1.call-update) | async-done | bytes 1966096 | tf_op jit(solution)/shard_map/reduce_scatter | solution.py:104
  (33 shorter events, 0.7 us)
Async XLA Ops:
  6.5 388.4 %all-reduce.3.cloned.1.call-start = ((), (), s32[]{:S(2)}) async-start(), calls=%async_computation.2 | async-start | bytes 7864320 | tf_op jit(solution)/shard_map/psum | solution.py:18
  6.5 114.2 %collective-permute-start.1 = (bf16[768,1280]{1,0:T(8,128)(2,1)}, bf16[768,1280]{1,0:T(8,128)(2,1)}, u32[]{:S(2)}, u32[]{:S(2)}) collective-permute-start(bf16[768,1280]{1,0:T(8,128)(2,1)} %param.8), channel_id=1, source_target_pairs={{0,4},{4,8},{8,12},{12,16},{16,20},{20,24},{24,28},{28,32},{32,36}... | collective-permute-start | bytes 5898248 | tf_op jit(solution)/shard_map/ppermute | solution.py:13
  30.3 9.5 %copy-start.11 = (s32[32]{0:T(128)S(1)}, s32[32]{0:T(128)}, u32[]{:S(2)}) copy-start(s32[32]{0:T(128)} %param.10) | copy-start | bytes 388
  34.7 5.2 copy-start.2
  36.7 88.1 %collective-permute-start = (bf16[768,1280]{0,1:T(8,128)(2,1)}, bf16[768,1280]{0,1:T(8,128)(2,1)}, u32[]{:S(2)}, u32[]{:S(2)}) collective-permute-start(bf16[768,1280]{0,1:T(8,128)(2,1)} %convert_element_type.83), channel_id=1, source_target_pairs={{0,4},{4,8},{8,12},{12,16},{16,20},{20,24},{24,28},{28,32},{32,36}... | collective-permute-start | bytes 5898248 | tf_op jit(solution)/shard_map/ppermute | solution.py:13
  42.6 17.1 %copy-start.1 = (bf16[768,1280]{0,1:T(8,128)(2,1)}, bf16[768,1280]{0,1:T(8,128)(2,1)S(1)}, u32[]{:S(2)}) copy-start(bf16[768,1280]{0,1:T(8,128)(2,1)S(1)} %copy.22) | copy-start | bytes 5898244
  49.7 496.1 %reduce-scatter.2.cloned.1.call-start = ((), (), s32[]{:S(2)}) async-start(), calls=%async_computation.1 | async-start | bytes 9830400 | tf_op jit(solution)/shard_map/reduce_scatter | solution.py:104
  137.4 10.9 %copy-start.6 = (f32[10,768]{1,0:T(8,128)}, f32[10,768]{1,0:T(8,128)S(1)}, u32[]{:S(2)}) copy-start(f32[10,768]{1,0:T(8,128)S(1)} %get-tuple-element.21) | copy-start | bytes 92164
  400.3 8.6 %copy-start = (f32[10,768,768]{1,2,0:T(8,128)}, f32[10,768,768]{1,2,0:T(8,128)S(1)}, u32[]{:S(2)}) copy-start(f32[10,768,768]{1,2,0:T(8,128)S(1)} %get-tuple-element.18) | copy-start | bytes 70778880
  400.3 8.6 %copy-start.4 = (bf16[768,10,128]{0,2,1:T(8,128)(2,1)S(1)}, bf16[768,10,128]{0,2,1:T(8,128)(2,1)}, u32[]{:S(2)}) copy-start(bf16[768,10,128]{0,2,1:T(8,128)(2,1)} %get-tuple-element.5) | copy-start | bytes 5898244
  408.9 10.0 %copy-start.5 = (f32[10,768]{1,0:T(8,128)S(1)}, f32[10,768]{1,0:T(8,128)}, u32[]{:S(2)}) copy-start(f32[10,768]{1,0:T(8,128)} %get-tuple-element.17) | copy-start | bytes 92164
  408.9 10.0 %copy-start.7 = (f32[10,768]{1,0:T(8,128)S(1)}, f32[10,768]{1,0:T(8,128)}, u32[]{:S(2)}) copy-start(f32[10,768]{1,0:T(8,128)} %copy-done.6) | copy-start | bytes 92164
  408.9 10.0 %copy-start.8 = (f32[10,768]{1,0:T(8,128)S(1)}, f32[10,768]{1,0:T(8,128)}, u32[]{:S(2)}) copy-start(f32[10,768]{1,0:T(8,128)} %convert_reduce_fusion.2) | copy-start | bytes 92164
  408.9 10.1 %copy-start.9 = (f32[10,768]{1,0:T(8,128)S(1)}, f32[10,768]{1,0:T(8,128)}, u32[]{:S(2)}) copy-start(f32[10,768]{1,0:T(8,128)} %convert_reduce_fusion.1) | copy-start | bytes 92164
  408.9 10.1 %copy-start.10 = (f32[10,768]{1,0:T(8,128)S(1)}, f32[10,768]{1,0:T(8,128)}, u32[]{:S(2)}) copy-start(f32[10,768]{1,0:T(8,128)} %convert_reduce_fusion) | copy-start | bytes 92164
  408.9 10.1 %copy-start.3 = (f32[10,768,128]{1,2,0:T(8,128)S(1)}, f32[10,768,128]{1,2,0:T(8,128)}, u32[]{:S(2)}) copy-start(f32[10,768,128]{1,2,0:T(8,128)} %fusion.4) | copy-start | bytes 11796484
Sparse Core Ops, SparseCore 0:
  49.8 345.0 all-reduce.2
  448.8 96.8 reduce-scatter.1
where the time goes:
time: 561 us; the launch traced here: 553 us
  waiting for transfers between devices  344 us (61%)
  matrix products  85.1 us (15%)
  other arithmetic  56.8 us (10%)
  local copies, waits for them, and re-layouts  43.5 us (8%)
  between operations  14.8 us (3%)
  starting transfers between devices  9.09 us (2%)
    psum x1, waiting for transfers between devices, broadcast(): return lax.psum(kept, axis)  247 us
    reduce_scatter x1, waiting for transfers between devices, shards(): lax.psum_scatter(terms.astype(jnp.bfloat16), 'head', scatter_dimension=1,...  97 us
    dot_general x3, matrix products, attend_block(): jnp.einsum('hqk,khd->hqd', weights, vh, preferred_element_type=jnp.float32)  36.5 us
    dot_general x3, matrix products, attend_block(): jnp.einsum('qhd,khd->hqk', qh, kh, preferred_element_type=jnp.float32)  30.8 us
    reduce_sum x3, other arithmetic, attend_block(): total = jnp.sum(weights.astype(jnp.float32), axis=-1)  28.7 us
    reshape x4, local copies, waits for them, and re-layouts, rotate(): parts = block.astype(jnp.float32).reshape(count, heads_here, HDIM // 2, 2)  19.7 us
    dot_general x1, matrix products, shards(): terms = jnp.dot(attended, out_weight, preferred_element_type=jnp.float32)  17.9 us
    convert_element_type x3, local copies, waits for them, and re-layouts, rotate(): jnp.stack([first, second], axis=-1).reshape(count, heads_here * HDIM)  11.6 us
  transfers between devices with their start and end apart: 4, of which 2 were waited for; matrix products, arithmetic and copies ran while one was open for 24% of the time, Pallas kernels for 0%

commit v1 on v0

--- a/solution.py
+++ b/solution.py
@@ -5,6 +5,12 @@
 
 HDIM = 128
 GRID_W = 32
+
+
+def gather_and_add(x, axis):
+    parts = lax.all_gather(x, axis, axis=0, tiled=False)
+    total = parts.sum(axis=0)
+    return total
 
 
 def shifted(array, axis, by):
@@ -15,7 +21,7 @@
 
 def broadcast(value, axis, source):
     kept = jnp.where(lax.axis_index(axis) == source, value, 0).astype(value.dtype)
-    return lax.psum(kept, axis)
+    return gather_and_add(kept, axis)
 
 
 def pair_angles(frame_value, count):

time: 561 us -> 1180 us (2.10)
  waiting for transfers between devices: 344 us -> 889 us
  other arithmetic: 56.8 us -> 107 us
    all_gather x0 -> x2, waiting for transfers between devices: none -> 807 us  [gather_and_add(): parts = lax.all_gather(x, axis, axis=0, tiled=False)]
    psum x1 -> x0, waiting for transfers between devices: 247 us -> none  [broadcast(): return lax.psum(kept, axis)]
    reduce_sum x0 -> x2, other arithmetic: none -> 45.5 us  [gather_and_add(): total = parts.sum(axis=0)]
    reduce_scatter x1, waiting for transfers between devices: 97 us -> 74.1 us  [shards(): lax.psum_scatter(terms.astype(jnp.bfloat16), 'head', scatter_dimension=1,...]
  transfers between devices with their start and end apart: 4 -> 5, of which waited for: 2 -> 4; matrix products, arithmetic and copies ran while one was open for 24% -> 14% of each run, Pallas kernels for 0% -> 0%
where the time goes in v1:
time: 1180 us; the launch traced here: 1170 us
  waiting for transfers between devices  889 us (75%)
  other arithmetic  107 us (9%)
  matrix products  93.8 us (8%)
  local copies, waits for them, and re-layouts  51.4 us (4%)
  between operations  16.5 us (1%)
    all_gather x2, waiting for transfers between devices, gather_and_add(): parts = lax.all_gather(x, axis, axis=0, tiled=False)  807 us
    reduce_scatter x1, waiting for transfers between devices, shards(): lax.psum_scatter(terms.astype(jnp.bfloat16), 'head', scatter_dimension=1,...  74.1 us
    reduce_sum x2, other arithmetic, gather_and_add(): total = parts.sum(axis=0)  45.5 us
    dot_general x3, matrix products, attend_block(): jnp.einsum('qhd,khd->hqk', qh, kh, preferred_element_type=jnp.float32)  40 us
    dot_general x3, matrix products, attend_block(): jnp.einsum('hqk,khd->hqd', weights, vh, preferred_element_type=jnp.float32)  35.9 us
    reduce_sum x3, other arithmetic, attend_block(): total = jnp.sum(weights.astype(jnp.float32), axis=-1)  31.7 us
  transfers between devices with their start and end apart: 5, of which 4 were waited for; matrix products, arithmetic and copies ran while one was open for 14% of the time, Pallas kernels for 0%

profile of v1, /device:TPU:1, one launch (start us, length us, event | category | flops | bytes accessed | tf_op | source)
XLA Modules:
  0.0 1167.9 jit_solution(10342810720730839764)
XLA Ops:
  13.6 5.6 reshape.290
  20.1 7.5 multiply_subtract_fusion
  27.5 6.3 broadcast_select_fusion
  33.8 5.3 select_n.175
  39.1 4.0 copy.67
  43.2 5.3 collective-permute-start.1
  50.2 5.3 collective-permute-start
  57.2 4.2 copy.59
  61.4 5.6 reshape.288
  67.0 7.1 subtract_convert_fusion
  74.1 5.7 pad_maximum_fusion
  79.8 4.5 convert_element_type.91
  84.3 12.6 %multiply_reduce_fusion.2 = (f32[10,768]{1,0:T(8,128)S(1)}, f32[10,768,768]{1,2,0:T(8,128)}) fusion(bf16[768,10,128]{0,2,1:T(8,128)(2,1)S(1)} %convert_element_type.91, bf16[768,10,128]{0,2,1:T(8,128)(2,1)} %convert_element_type.93), kind=kOutput, calls=%fused_computation.8 | convolution fusion | flops 1521738240 | bytes 27555840 | tf_op jit(solution)/shard_map/qhd,khd->hqk/dot_general | solution.py:75
  97.0 10.6 convert_reduce_fusion.2
  107.6 4.0 copy.63
  111.5 14.7 %fusion.4 = f32[10,768,128]{1,2,0:T(8,128)} fusion(bf16[768,10,128]{0,2,1:T(8,128)(2,1)} %bitcast.110, f32[10,768,768]{1,2,0:T(8,128)} %get-tuple-element.20, f32[10,768]{1,0:T(8,128)S(1)} %get-tuple-element.19), kind=kOutput, calls=%fused_computation.25 | convolution fusion | flops 1527644160 | bytes 29521920 | tf_op jit(solution)/shard_map/hqk,khd->hqd/dot_general | solution.py:81
  126.2 4.0 copy.71
  130.2 7.4 collective-permute-done
  137.6 14.8 %multiply_reduce_fusion.1 = (f32[10,768]{1,0:T(8,128)S(1)}, f32[10,768,768]{1,2,0:T(8,128)}) fusion(bf16[768,10,128]{0,2,1:T(8,128)(2,1)S(1)} %convert_element_type.91, bf16[768,10,128]{0,2,1:T(8,128)(2,1)} %bitcast.5), kind=kOutput, calls=%fused_computation.7 | convolution fusion | flops 1521738240 | bytes 27555840 | tf_op jit(solution)/shard_map/qhd,khd->hqk/dot_general | solution.py:75
  152.3 11.0 convert_reduce_fusion.1
  163.3 383.6 %all-gather.6.cloned.1.call-done = bf16[24576,1280]{1,0:T(8,128)(2,1)} async-done(((bf16[768,1280]{1,0:T(8,128)(2,1)}), bf16[24576,1280]{1,0:T(8,128)(2,1)}) %all-gather.6.cloned.1.call-update) | async-done | bytes 62914576 | tf_op jit(solution)/shard_map/all_gather | solution.py:11
  546.9 23.7 %reduce_sum.58 = bf16[768,1280]{1,0:T(8,128)(2,1)} reduce(bf16[32,768,1280]{2,1,0:T(8,128)(2,1)} %bitcast.108, bf16[]{:T(256)} %constant.89.clone.1), dimensions={0}, to_apply=%region_4.5 | reduce | flops 30474240 | bytes 64880640 | tf_op jit(solution)/shard_map/reduce_sum | solution.py:12
  570.6 4.0 copy.73
  574.7 423.7 %all-gather.4.cloned.1.call-done = bf16[32,768,1280]{2,1,0:T(8,128)(2,1)} async-done(((bf16[1,768,1280]{2,1,0:T(8,128)(2,1)}), bf16[32,768,1280]{2,1,0:T(8,128)(2,1)}) %all-gather.4.cloned.1.call-update) | async-done | bytes 62914576 | tf_op jit(solution)/shard_map/all_gather | solution.py:11
  998.3 21.7 %reduce_sum.57 = bf16[768,1280]{1,0:T(8,128)(2,1)} reduce(bf16[32,768,1280]{2,1,0:T(8,128)(2,1)} %all-gather.4.cloned.1.call-done, bf16[]{:T(256)} %constant.89.clone.1), dimensions={0}, to_apply=%region_2.3 | reduce | flops 30474240 | bytes 64880640 | tf_op jit(solution)/shard_map/reduce_sum | solution.py:12
  1020.1 4.1 copy.68
  1024.2 12.6 %multiply_reduce_fusion = (f32[10,768]{1,0:T(8,128)S(1)}, f32[10,768,768]{1,2,0:T(8,128)}) fusion(bf16[768,10,128]{0,2,1:T(8,128)(2,1)S(1)} %convert_element_type.91, bf16[768,10,128]{0,2,1:T(8,128)(2,1)} %bitcast.111), kind=kOutput, calls=%fused_computation.6 | convolution fusion | flops 1521738240 | bytes 27555840 | tf_op jit(solution)/shard_map/qhd,khd->hqk/dot_general | solution.py:75
  1036.8 10.1 convert_reduce_fusion
  1047.0 9.9 fusion.5
  1057.6 11.3 fusion.2
  1069.0 17.9 %convolution_convert_fusion = bf16[768,5120]{1,0:T(8,128)(2,1)} fusion(bf16[768,1280]{0,1:T(8,128)(2,1)} %bitcast.116, bf16[1280,5120]{1,0:T(8,128)(2,1)} %param.9), kind=kOutput, calls=%fused_computation.9 | convolution fusion | flops 10070261760 | bytes 22937600 | tf_op jit(solution)/shard_map/dot_general | solution.py:109
  1086.9 74.1 %reduce-scatter.2.cloned.1.call-done = bf16[768,1280]{1,0:T(8,128)(2,1)} async-done(((bf16[768,5120]{1,0:T(8,128)(2,1)}), bf16[768,1280]{1,0:T(8,128)(2,1)}) %reduce-scatter.2.cloned.1.call-update) | async-done | bytes 1966096 | tf_op jit(solution)/shard_map/reduce_scatter | solution.py:110
  (32 shorter events, 9.4 us)
Async XLA Ops:
  6.5 4.2 copy-start.2
  6.5 540.4 %all-gather.6.cloned.1.call-start = ((), (), s32[]{:S(2)}) async-start(), calls=%async_computation.3 | async-start | bytes 64880640 | tf_op jit(solution)/shard_map/all_gather | solution.py:11
  10.1 988.3 %all-gather.4.cloned.1.call-start = ((), (), s32[]{:S(2)}) async-start(), calls=%async_computation.1 | async-start | bytes 64880640 | tf_op jit(solution)/shard_map/all_gather | solution.py:11
  43.1 1117.9 %reduce-scatter.2.cloned.1.call-start = ((), (), s32[]{:S(2)}) async-start(), calls=%async_computation.2 | async-start | bytes 9830400 | tf_op jit(solution)/shard_map/reduce_scatter | solution.py:110
  43.2 83.1 %collective-permute-start.1 = (bf16[768,1280]{1,0:T(8,128)(2,1)}, bf16[768,1280]{1,0:T(8,128)(2,1)}, u32[]{:S(2)}, u32[]{:S(2)}) collective-permute-start(bf16[768,1280]{1,0:T(8,128)(2,1)} %param.8), channel_id=1, source_target_pairs={{0,4},{4,8},{8,12},{12,16},{16,20},{20,24},{24,28},{28,32},{32,36}... | collective-permute-start | bytes 5898248 | tf_op jit(solution)/shard_map/ppermute | solution.py:19
  50.2 87.4 %collective-permute-start = (bf16[768,1280]{0,1:T(8,128)(2,1)}, bf16[768,1280]{0,1:T(8,128)(2,1)}, u32[]{:S(2)}, u32[]{:S(2)}) collective-permute-start(bf16[768,1280]{0,1:T(8,128)(2,1)} %convert_element_type.95), channel_id=1, source_target_pairs={{0,4},{4,8},{8,12},{12,16},{16,20},{20,24},{24,28},{28,32},{32,36}... | collective-permute-start | bytes 5898248 | tf_op jit(solution)/shard_map/ppermute | solution.py:19
  152.3 11.0 copy-start.4
  1036.8 10.1 copy-start
  1046.9 10.0 copy-start.5
  1046.9 10.0 copy-start.6
  1046.9 10.0 copy-start.7
  1046.9 10.7 copy-start.1
  1046.9 10.7 copy-start.3
Sparse Core Ops, SparseCore 0:
  10.4 536.4 all-gather.5
  549.9 448.3 all-gather.3
  1087.0 73.9 reduce-scatter.1
